TPU v7x, 512 devices: a whole 4x8x8 slice. The times are simulated.
512 devices in a mesh: kv: 16 (over z, core), ep: 32 (over x, y).
Axes of the slice: x: 4, y: 8, z: 8, core: 2. Of those that a mesh axis runs over, the one named last changes fastest.
Arguments:
- queries: bfloat16 [32, 64, 2048], P('ep'), may hold values from -12 to 12
- new_keys: bfloat16 [32, 64, 512], P('ep'), may hold values from -12 to 12
- new_values: bfloat16 [32, 64, 512], P('ep'), may hold values from -6 to 6
- cache_keys: bfloat16 [32, 64, 128, 512], P('ep', 'kv'), may hold values from -12 to 12
- cache_values: bfloat16 [32, 64, 128, 512], P('ep', 'kv'), may hold values from -10 to 10
- page_table: int32 [32, 64], P('ep'), may hold values from 0 to 63, each once within a row
- cached_len: int32 [32], P('ep'), may hold values from 1 to 8192, 65536 in all
- moe_rows: bfloat16 [1024, 4096], P('ep'), may hold values from -6 to 6
- expert_ids: int32 [1024, 2], P('ep'), may hold values from 0 to 7, all different within a row; in each aligned block of 32 rows (0 to 31, 32 to 63, ...) at most 16 rows name the same one
- gate_probs: float32 [1024, 2], P('ep'), may hold values from 0.1 to 0.9
- w_gate: bfloat16 [32, 4096, 2048], P('ep', None, 'kv'), may hold values from -0.09375 to 0.09375
- w_up: bfloat16 [32, 4096, 2048], P('ep', None, 'kv'), may hold values from -0.09375 to 0.09375
- w_down: bfloat16 [32, 2048, 4096], P('ep', 'kv'), may hold values from -0.09375 to 0.09375
Outputs:
- attn_out: bfloat16 [32, 64, 2048], P('ep')
- moe_out: bfloat16 [1024, 4096], P('ep', 'kv')
Inputs may be any that keep to these rules, and one draw needn't show every extreme that they name: `page_table`: each row is a permutation of the 64 slots of its request. `cached_len`: cached positions at or past a request's length hold no data. `expert_ids`: each row names 2 different experts; among the 32 rows of one ep index no expert is named more than 16 times, and this bound is reached.
All inputs are finite; a program needn't handle non-finite values. No bound on the sum of `cached_len` on one device may be relied on, other than what follows from the above.
Results may differ from a plain program's by a relative error of at most 0.0085.
Values may be sent and summed in bfloat16 or wider, within the bound.
No kernel may reach another device: no remote copies, remote signals or barrier semaphores. Data moves between devices by JAX's collectives and lax.ppermute only.
A program may use at most 128 MiB of HBM per device.

v0:
```python
import math
import jax
import jax.numpy as jnp
from jax import lax
from jax.sharding import PartitionSpec as P

HD = 128
EXPERTS = 8
TOP = 2
HQ = 16
KVH = 4
PAGE = 128
POOL_DEV = 4
CAP = 16
ROPE_BASE = 10000.0
MASKED = -1e30


def rotary(values, positions):
    half_width = values.shape[-1] // 2
    indices = jnp.arange(half_width, dtype=jnp.float32)
    frequency = jnp.power(ROPE_BASE, -2.0 * indices / values.shape[-1])
    angles = positions.astype(jnp.float32)[:, None] * frequency[None, :]
    cosine = jnp.cos(angles)[:, None, :]
    sine_part = jnp.sin(angles)[:, None, :]
    lower_half = values[..., :half_width]
    upper_half = values[..., half_width:]
    return jnp.concatenate(
        [
            lower_half * cosine - upper_half * sine_part,
            upper_half * cosine + lower_half * sine_part,
        ],
        axis=-1,
    )


def on_device(
    queries,
    new_keys,
    new_values,
    cache_keys,
    cache_values,
    page_table,
    cached_len,
    moe_rows,
    expert_ids,
    gate_probs,
    w_gate,
    w_up,
    w_down,
):
    kv_index = lax.axis_index("kv")
    kv_count = lax.axis_size("kv")
    all_rows = queries.shape[1]
    block_rows = all_rows // kv_count
    length = cached_len[0]
    group_size = HQ // KVH
    score_scale = 1.0 / math.sqrt(HD)
    slot_ids = kv_index * POOL_DEV + jnp.arange(POOL_DEV, dtype=jnp.int32)
    matches = (page_table[0][:, None] == slot_ids[None, :]).astype(jnp.int32)
    page_index = jnp.sum(
        matches * jnp.arange(page_table.shape[1], dtype=jnp.int32)[:, None], axis=0
    )
    cached_pos = (page_index[:, None] * PAGE + jnp.arange(PAGE, dtype=jnp.int32)[None, :]).reshape(
        -1
    )
    block_start = kv_index * block_rows
    own_pos = length + block_start + jnp.arange(block_rows, dtype=jnp.int32)
    key_block = lax.dynamic_slice_in_dim(new_keys[0], block_start, block_rows, 0)
    value_block = lax.dynamic_slice_in_dim(new_values[0], block_start, block_rows, 0)
    own_keys = rotary(key_block.astype(jnp.float32).reshape(block_rows, KVH, HD), own_pos).astype(
        jnp.bfloat16
    )
    local_keys = jnp.concatenate([cache_keys[0].reshape(-1, KVH, HD), own_keys], axis=0)
    local_values = jnp.concatenate(
        [cache_values[0].reshape(-1, KVH, HD), value_block.reshape(block_rows, KVH, HD)], axis=0
    )
    key_pos = jnp.concatenate([cached_pos, own_pos])
    live_keys = jnp.concatenate([cached_pos < length, jnp.ones((block_rows,), jnp.bool_)])
    positions = length + jnp.arange(all_rows, dtype=jnp.int32)
    rotated = rotary(queries[0].astype(jnp.float32).reshape(all_rows, HQ, HD), positions).astype(
        jnp.bfloat16
    )
    grouped = rotated.reshape(all_rows, KVH, group_size, HD)
    scores = (
        jnp.einsum("nkgd,mkd->nkgm", grouped, local_keys, preferred_element_type=jnp.float32)
        * score_scale
    )
    usable = (live_keys[None, :] & (key_pos[None, :] <= positions[:, None]))[:, None, None, :]
    scores = jnp.where(usable, scores, MASKED)
    part_high = jnp.max(scores, axis=-1)
    highest = lax.pmax(part_high, "kv")
    weights = jnp.where(usable, jnp.exp(scores - highest[..., None]), 0.0)
    part_total = jnp.sum(weights, axis=-1)
    part_blend = jnp.einsum(
        "nkgm,mkd->nkgd",
        weights.astype(jnp.bfloat16),
        local_values,
        preferred_element_type=jnp.float32,
    )
    total_row = jnp.pad(part_total.reshape(1, -1), ((0, 0), (0, HQ * HD - all_rows * HQ)))
    packed = lax.psum(
        jnp.concatenate([part_blend.reshape(all_rows, HQ * HD), total_row], axis=0), "kv"
    )
    row_total = packed[all_rows, : all_rows * HQ].reshape(all_rows, HQ)
    blended = packed[:all_rows].reshape(all_rows, HQ, HD)
    attn_out = (blended / row_total[..., None]).reshape(1, all_rows, HQ * HD).astype(jnp.bfloat16)
    ep_count = lax.axis_size("ep")
    share_count = ep_count // EXPERTS
    tok_rows = moe_rows.shape[0]
    slot_total = ep_count * CAP
    flat_ids = expert_ids.reshape(-1)
    one_hot = (flat_ids[:, None] == jnp.arange(EXPERTS, dtype=jnp.int32)[None, :]).astype(jnp.int32)
    earlier = jnp.cumsum(one_hot, axis=0) - one_hot
    slot_rank = jnp.sum(earlier * one_hot, axis=1)
    slot_index = jnp.arange(slot_total, dtype=jnp.int32)
    dest_expert = slot_index // CAP // share_count
    dest_slot = slot_index % CAP
    matched = (flat_ids[None, :] == dest_expert[:, None]) & (
        slot_rank[None, :] == dest_slot[:, None]
    )
    select = jnp.sum(matched.astype(jnp.float32).reshape(slot_total, tok_rows, TOP), axis=2).astype(
        jnp.bfloat16
    )
    weight_map = jnp.sum(
        jnp.where(matched, gate_probs.reshape(-1)[None, :], 0.0).reshape(slot_total, tok_rows, TOP),
        axis=2,
    )
    col_width = moe_rows.shape[1] // kv_count
    rows_cols = lax.dynamic_slice_in_dim(moe_rows, kv_index * col_width, col_width, 1)
    outgoing = (
        jnp.dot(select, rows_cols, preferred_element_type=jnp.float32)
        .astype(jnp.bfloat16)
        .reshape(ep_count, CAP, -1)
    )
    arrived_cols = lax.all_to_all(outgoing, "ep", split_axis=0, concat_axis=0, tiled=True).reshape(
        slot_total, -1
    )
    arrived = lax.all_gather(arrived_cols, "kv", axis=1, tiled=True)
    gate_proj = jnp.dot(arrived, w_gate[0], preferred_element_type=jnp.float32)
    up_proj = jnp.dot(arrived, w_up[0], preferred_element_type=jnp.float32)
    hidden = (jax.nn.silu(gate_proj) * up_proj).astype(jnp.bfloat16)
    out_width = w_down.shape[2] // kv_count
    down_split = w_down[0].reshape(w_down.shape[1], kv_count, out_width)
    down_cols = lax.all_to_all(down_split, "kv", split_axis=1, concat_axis=0, tiled=True).reshape(
        -1, out_width
    )
    summed = jnp.dot(
        lax.all_gather(hidden, "kv", axis=1, tiled=True),
        down_cols,
        preferred_element_type=jnp.float32,
    )
    returned = (
        lax.all_to_all(
            summed.reshape(ep_count, CAP, -1).astype(jnp.bfloat16),
            "ep",
            split_axis=0,
            concat_axis=0,
            tiled=True,
        )
        .astype(jnp.float32)
        .reshape(slot_total, -1)
    )
    moe_out = jnp.dot(
        weight_map.T, returned, precision=lax.Precision.HIGHEST, preferred_element_type=jnp.float32
    ).astype(jnp.bfloat16)
    return (attn_out, moe_out)


def solution(mesh):
    return jax.shard_map(
        on_device,
        mesh=mesh,
        in_specs=(
            P("ep", None, None),
            P("ep", None, None),
            P("ep", None, None),
            P("ep", "kv", None, None),
            P("ep", "kv", None, None),
            P("ep", None),
            P("ep"),
            P("ep", None),
            P("ep", None),
            P("ep", None),
            P("ep", None, "kv"),
            P("ep", None, "kv"),
            P("ep", "kv", None),
        ),
        out_specs=(P("ep", None, None), P("ep", "kv")),
        check_vma=False,
    )
```

profile of v0, /device:TPU:2, one launch (start us, length us, event | category | flops | bytes accessed | tf_op | source)
XLA Modules:
  0.0 277.6 jit_solution(767339811898479776)
XLA Ops:
  7.2 0.8 copy.46
  8.7 0.8 convert_reduce_fusion
  9.6 1.0 convolution_convert_fusion
  10.5 21.4 %all_to_all.25 = bf16[32,16,256]{2,1,0:T(8,128)(2,1)} all-to-all(bf16[32,16,256]{2,1,0:T(8,128)(2,1)S(1)} %bitcast.94), channel_id=1, replica_groups=mesh['kv'=16,'ep'=32] {'ep'}, dimensions={0} | all-to-all | bytes 524288 | tf_op jit(solution)/shard_map/all_to_all | solution.py:136
  32.0 1.5 copy.55
  33.5 1.3 copy.48
  34.8 10.5 %all-to-all-start.1 = ((bf16[128,16,256]{2,0,1:T(8,128)(2,1)}), bf16[128,16,256]{2,0,1:T(8,128)(2,1)S(1)}, u32[]{:S(2)}, u32[]{:S(2)}) async-start(bf16[128,16,256]{2,0,1:T(8,128)(2,1)} %copy.48), calls=%async_computation.1 | async-start | bytes 2097152 | tf_op jit(solution)/shard_map/all_to_all | solution.py:145
  46.2 1.2 reshape_squeeze.10
  47.4 0.9 copy.41
  48.5 55.1 %all-gather.3.cloned.1.call-done = bf16[512,4096]{1,0:T(8,128)(2,1)} async-done(((bf16[512,256]{1,0:T(8,128)(2,1)}), bf16[512,4096]{1,0:T(8,128)(2,1)}) %all-gather.3.cloned.1.call-update) | async-done | bytes 4194320 | tf_op jit(solution)/shard_map/all_gather | solution.py:139
  103.5 3.6 %fusion.11 = f32[512,128]{1,0:T(8,128)S(1)} fusion(bf16[512,4096]{1,0:T(8,128)(2,1)} %all-gather.3.cloned.1.call-done, bf16[1,4096,128]{2,1,0:T(8,128)(2,1)S(1)} %copy-done), kind=kOutput, calls=%fused_computation.14 | convolution fusion | flops 536870912 | bytes 5505024 | tf_op jit(solution)/shard_map/dot_general | solution.py:140
  107.3 1.9 fusion.9
  111.2 2.2 fusion
  113.5 24.3 %pmax.7 = f32[64,4,4]{0,2,1:T(4,128)S(1)} all-reduce(f32[64,4,4]{0,2,1:T(4,128)S(1)} %get-tuple-element.14), channel_id=1, replica_groups=mesh['kv'=16,'ep'=32] {'kv'}, use_global_device_ids=true, to_apply=%region_2.3 | all-reduce | flops 1024 | bytes 8192 | tf_op jit(solution)/shard_map/pmax | solution.py:92
  137.8 2.6 fusion.1
  141.6 2.5 fusion.6
  144.7 0.9 select_maximum_fusion
  145.6 3.0 %all-gather.5.cloned.1.call-done = bf16[512,2048]{1,0:T(8,128)(2,1)} async-done(((bf16[512,128]{1,0:T(8,128)(2,1)}), bf16[512,2048]{1,0:T(8,128)(2,1)}) %all-gather.5.cloned.1.call-update) | async-done | bytes 2097168 | tf_op jit(solution)/shard_map/all_gather | solution.py:149
  148.6 3.0 %convolution_convert_fusion.1 = bf16[32,16,256]{2,1,0:T(8,128)(2,1)} fusion(bf16[32,16,2048]{2,1,0:T(8,128)(2,1)} %bitcast.97, bf16[2048,256,1]{1,0,2:T(8,128)(2,1)S(1)} %bitcast.91), kind=kOutput, calls=%fused_computation.9 | convolution fusion | flops 537001984 | bytes 3407872 | tf_op jit(solution)/shard_map/dot_general | solution.py:148
  151.6 9.9 %all-to-all-start.2 = ((bf16[32,16,256]{2,1,0:T(8,128)(2,1)}), bf16[32,16,256]{2,1,0:T(8,128)(2,1)S(1)}, u32[]{:S(2)}, u32[]{:S(2)}) async-start(bf16[32,16,256]{2,1,0:T(8,128)(2,1)} %convolution_convert_fusion.1), calls=%async_computation.2 | async-start | bytes 524288 | tf_op jit(solution)/shard_map/all_to_all | solution.py:154
  161.5 105.7 %all-reduce.4.cloned.1.call-done = f32[65,2048]{1,0:T(8,128)} async-done(((f32[65,2048]{1,0:T(8,128)}), f32[65,2048]{1,0:T(8,128)}) %all-reduce.4.cloned.1.call-update) | async-done | bytes 532496 | tf_op jit(solution)/shard_map/psum | solution.py:102
  267.2 0.8 slice_reduce_fusion
  268.2 1.9 fusion.24
  270.2 0.9 convolution_convert_fusion.2
  (57 shorter events, 5.3 us)
Async XLA Ops:
  7.2 96.4 %copy-start = (bf16[1,4096,128]{2,1,0:T(8,128)(2,1)S(1)}, bf16[1,4096,128]{2,1,0:T(8,128)(2,1)}, u32[]{:S(2)}) copy-start(bf16[1,4096,128]{2,1,0:T(8,128)(2,1)} %param.23) | copy-start | bytes 3145732
  7.2 96.3 %all-gather.3.cloned.1.call-start = ((), (), s32[]{:S(2)}) async-start(), calls=%async_computation.4 | async-start | bytes 4456448 | tf_op jit(solution)/shard_map/all_gather | solution.py:139
  33.5 12.6 %copy-start.4 = (bf16[1,64,2048]{2,1,0:T(8,128)(2,1)S(1)}, bf16[1,64,2048]{2,1,0:T(8,128)(2,1)}, u32[]{:S(2)}) copy-start(bf16[1,64,2048]{2,1,0:T(8,128)(2,1)} %param.13) | copy-start | bytes 786436
  34.8 13.5 %copy-start.6 = (s32[1,64]{1,0:T(1,128)S(1)}, s32[1,64]{1,0:T(1,128)}, u32[]{:S(2)}) copy-start(s32[1,64]{1,0:T(1,128)} %param.18) | copy-start | bytes 772
  34.8 110.8 %all-to-all-start.1 = ((bf16[128,16,256]{2,0,1:T(8,128)(2,1)}), bf16[128,16,256]{2,0,1:T(8,128)(2,1)S(1)}, u32[]{:S(2)}, u32[]{:S(2)}) async-start(bf16[128,16,256]{2,0,1:T(8,128)(2,1)} %copy.48), calls=%async_computation.1 | async-start | bytes 2097152 | tf_op jit(solution)/shard_map/all_to_all | solution.py:145
  45.4 103.2 %all-gather.5.cloned.1.call-start = ((), (), s32[]{:S(2)}) async-start(), calls=%async_computation.5 | async-start | bytes 2228224 | tf_op jit(solution)/shard_map/all_gather | solution.py:149
  103.5 3.6 %copy-start.1 = (bf16[512,4096]{1,0:T(8,128)(2,1)S(1)}, bf16[512,4096]{1,0:T(8,128)(2,1)}, u32[]{:S(2)}) copy-start(bf16[512,4096]{1,0:T(8,128)(2,1)} %all-gather.3.cloned.1.call-done) | copy-start | bytes 12582916
  103.5 3.7 %copy-start.5 = (bf16[1,4096,128]{2,1,0:T(8,128)(2,1)S(1)}, bf16[1,4096,128]{2,1,0:T(8,128)(2,1)}, u32[]{:S(2)}) copy-start(bf16[1,4096,128]{2,1,0:T(8,128)(2,1)} %param.24) | copy-start | bytes 3145732
  109.2 2.0 copy-start.3
  109.2 158.0 %all-reduce.4.cloned.1.call-start = ((), (), s32[]{:S(2)}) async-start(), calls=%async_computation.3 | async-start | bytes 1179648 | tf_op jit(solution)/shard_map/psum | solution.py:102
  111.2 29.5 %copy-start.2 = (bf16[1,4,128,512]{3,2,1,0:T(8,128)(2,1)S(1)}, bf16[1,4,128,512]{3,2,1,0:T(8,128)(2,1)}, u32[]{:S(2)}) copy-start(bf16[1,4,128,512]{3,2,1,0:T(8,128)(2,1)} %param.17) | copy-start | bytes 1572868
  151.6 118.6 %all-to-all-start.2 = ((bf16[32,16,256]{2,1,0:T(8,128)(2,1)}), bf16[32,16,256]{2,1,0:T(8,128)(2,1)S(1)}, u32[]{:S(2)}, u32[]{:S(2)}) async-start(bf16[32,16,256]{2,1,0:T(8,128)(2,1)} %convolution_convert_fusion.1), calls=%async_computation.2 | async-start | bytes 524288 | tf_op jit(solution)/shard_map/all_to_all | solution.py:154
Sparse Core Ops, SparseCore 0:
  32.1 71.3 all-gather.2
  109.3 39.2 all-gather.4
  150.9 116.2 all-reduce.3
where the time goes:
time: 278 us
  waiting for transfers between devices  164 us (59%)
  blocking collectives  45.7 us (16%)
  starting transfers between devices  20.6 us (7%)
  matrix products  15 us (5%)
  between operations  14.7 us (5%)
  local copies, waits for them, and re-layouts  9.25 us (3%)
  other arithmetic  8.53 us (3%)
    psum x1, waiting for transfers between devices, on_device(): lax.psum(jnp.concatenate([part_blend.reshape(all_rows, HQ * HD), total_ro...  106 us
    all_gather x1, waiting for transfers between devices, on_device(): arrived = lax.all_gather(arrived_cols, 'kv', axis=1, tiled=True)  55.1 us
    pmax x1, blocking collectives, on_device(): highest = lax.pmax(part_high, 'kv')  24.3 us
    all_to_all x1, blocking collectives, on_device(): lax.all_to_all(outgoing, 'ep', split_axis=0, concat_axis=0, tiled=True)  21.4 us
    all_to_all x1, starting transfers between devices, on_device(): lax.all_to_all(down_split, 'kv', split_axis=1, concat_axis=0, tiled=True)  10.5 us
    all_to_all x1, starting transfers between devices, on_device(): lax.all_to_all(summed.reshape(ep_count, CAP, -1).astype(jnp.bfloat16), 'e...  9.89 us
  transfers between devices with their start and end apart: 5, of which 3 were waited for; matrix products, arithmetic and copies ran while one was open for 10% of the time, Pallas kernels for 0%

commit v1 on v0

--- a/solution.py
+++ b/solution.py
@@ -3,6 +3,7 @@
 import jax.numpy as jnp
 from jax import lax
 from jax.sharding import PartitionSpec as P
+from jax.lax import all_to_all, axis_size
 
 HD = 128
 EXPERTS = 8
@@ -14,6 +15,15 @@
 CAP = 16
 ROPE_BASE = 10000.0
 MASKED = -1e30
+
+
+def obtain_the_copies(array_in):
+    frame_out = axis_size("kv")
+    n_now = jnp.split(array_in, frame_out, axis=1)
+    field_out = jnp.stack(n_now, axis=0)
+    met_up = all_to_all(field_out, "kv", 0, 0)
+    shaped = jnp.concatenate(met_up, axis=0)
+    return shaped
 
 
 def rotary(values, positions):
@@ -142,9 +152,7 @@
     hidden = (jax.nn.silu(gate_proj) * up_proj).astype(jnp.bfloat16)
     out_width = w_down.shape[2] // kv_count
     down_split = w_down[0].reshape(w_down.shape[1], kv_count, out_width)
-    down_cols = lax.all_to_all(down_split, "kv", split_axis=1, concat_axis=0, tiled=True).reshape(
-        -1, out_width
-    )
+    down_cols = obtain_the_copies(down_split).reshape(-1, out_width)
     summed = jnp.dot(
         lax.all_gather(hidden, "kv", axis=1, tiled=True),
         down_cols,

time: 278 us -> 277 us (level)
  no operation moved by 1% of the time
where the time goes in v1:
time: 277 us; the launch traced here: 276 us
  waiting for transfers between devices  162 us (58%)
  blocking collectives  46.5 us (17%)
  starting transfers between devices  20.5 us (7%)
  matrix products  15 us (5%)
  between operations  14.8 us (5%)
  local copies, waits for them, and re-layouts  9.62 us (3%)
  other arithmetic  8.52 us (3%)
    psum x1, waiting for transfers between devices, on_device(): lax.psum(jnp.concatenate([part_blend.reshape(all_rows, HQ * HD), total_ro...  105 us
    all_gather x1, waiting for transfers between devices, on_device(): arrived = lax.all_gather(arrived_cols, 'kv', axis=1, tiled=True)  54.8 us
    pmax x1, blocking collectives, on_device(): highest = lax.pmax(part_high, 'kv')  25.1 us
    all_to_all x1, blocking collectives, on_device(): lax.all_to_all(outgoing, 'ep', split_axis=0, concat_axis=0, tiled=True)  21.4 us
    all_to_all x1, starting transfers between devices, obtain_the_copies(): met_up = all_to_all(field_out, 'kv', 0, 0)  10.5 us
    all_to_all x1, starting transfers between devices, on_device(): lax.all_to_all(summed.reshape(ep_count, CAP, -1).astype(jnp.bfloat16), 'e...  9.8 us
  transfers between devices with their start and end apart: 5, of which 3 were waited for; matrix products, arithmetic and copies ran while one was open for 10% of the time, Pallas kernels for 0%

profile of v1, /device:TPU:2, one launch (start us, length us, event | category | flops | bytes accessed | tf_op | source)
XLA Modules:
  0.0 276.5 jit_solution(16565439048841786690)
XLA Ops:
  7.2 0.8 copy.86
  8.7 0.8 convert_reduce_fusion
  9.6 1.0 convolution_convert_fusion
  10.5 21.4 %all_to_all.15 = bf16[32,16,256]{2,1,0:T(8,128)(2,1)} all-to-all(bf16[32,16,256]{2,1,0:T(8,128)(2,1)S(1)} %bitcast.166), channel_id=1, replica_groups=mesh['kv'=16,'ep'=32] {'ep'}, dimensions={0} | all-to-all | bytes 524288 | tf_op jit(solution)/shard_map/all_to_all | solution.py:146
  32.0 1.6 copy.88
  33.9 1.3 copy.89
  35.2 10.5 %all-to-all-start.1 = ((bf16[16,128,1,256]{3,1,2,0:T(8,128)(2,1)}), bf16[16,128,1,256]{3,1,2,0:T(8,128)(2,1)S(1)}, u32[]{:S(2)}, u32[]{:S(2)}) async-start(bf16[16,128,1,256]{3,1,2,0:T(8,128)(2,1)} %copy.89), calls=%async_computation.1 | async-start | bytes 2097152 | tf_op jit(solution)/shard_map/all_to_all | solution.py:24
  46.7 1.2 reshape_squeeze.10
  47.8 0.9 copy.81
  48.9 54.8 %all-gather.3.cloned.1.call-done = bf16[512,4096]{1,0:T(8,128)(2,1)} async-done(((bf16[512,256]{1,0:T(8,128)(2,1)}), bf16[512,4096]{1,0:T(8,128)(2,1)}) %all-gather.3.cloned.1.call-update) | async-done | bytes 4194320 | tf_op jit(solution)/shard_map/all_gather | solution.py:149
  103.7 3.6 %fusion.11 = f32[512,128]{1,0:T(8,128)S(1)} fusion(bf16[512,4096]{1,0:T(8,128)(2,1)} %all-gather.3.cloned.1.call-done, bf16[1,4096,128]{2,1,0:T(8,128)(2,1)S(1)} %copy-done), kind=kOutput, calls=%fused_computation.14 | convolution fusion | flops 536870912 | bytes 5505024 | tf_op jit(solution)/shard_map/dot_general | solution.py:150
  107.5 1.9 fusion.9
  111.4 2.2 fusion
  113.6 25.1 %pmax.7 = f32[64,4,4]{0,2,1:T(4,128)S(1)} all-reduce(f32[64,4,4]{0,2,1:T(4,128)S(1)} %get-tuple-element.14), channel_id=1, replica_groups=mesh['kv'=16,'ep'=32] {'kv'}, use_global_device_ids=true, to_apply=%region_2.3 | all-reduce | flops 1024 | bytes 8192 | tf_op jit(solution)/shard_map/pmax | solution.py:102
  138.7 2.6 fusion.1
  142.6 2.5 fusion.6
  145.7 0.9 select_maximum_fusion
  146.5 1.4 all-gather.5.cloned.1.call-done
  147.9 3.0 %convolution_convert_fusion.1 = bf16[32,16,256]{2,1,0:T(8,128)(2,1)} fusion(bf16[32,16,2048]{2,1,0:T(8,128)(2,1)} %bitcast.169, bf16[2048,256,1]{1,0,2:T(8,128)(2,1)S(1)} %bitcast.163), kind=kOutput, calls=%fused_computation.9 | convolution fusion | flops 537001984 | bytes 3407872 | tf_op jit(solution)/shard_map/dot_general | solution.py:156
  150.9 9.8 %all-to-all-start.2 = ((bf16[32,16,256]{2,1,0:T(8,128)(2,1)}), bf16[32,16,256]{2,1,0:T(8,128)(2,1)S(1)}, u32[]{:S(2)}, u32[]{:S(2)}) async-start(bf16[32,16,256]{2,1,0:T(8,128)(2,1)} %convolution_convert_fusion.1), calls=%async_computation.2 | async-start | bytes 524288 | tf_op jit(solution)/shard_map/all_to_all | solution.py:162
  160.7 105.4 %all-reduce.4.cloned.1.call-done = f32[65,2048]{1,0:T(8,128)} async-done(((f32[65,2048]{1,0:T(8,128)}), f32[65,2048]{1,0:T(8,128)}) %all-reduce.4.cloned.1.call-update) | async-done | bytes 532496 | tf_op jit(solution)/shard_map/psum | solution.py:112
  266.1 0.8 slice_reduce_fusion
  267.2 1.9 fusion.24
  269.1 0.9 convolution_convert_fusion.2
  (73 shorter events, 5.5 us)
Async XLA Ops:
  7.2 96.5 %copy-start = (bf16[1,4096,128]{2,1,0:T(8,128)(2,1)S(1)}, bf16[1,4096,128]{2,1,0:T(8,128)(2,1)}, u32[]{:S(2)}) copy-start(bf16[1,4096,128]{2,1,0:T(8,128)(2,1)} %param.23) | copy-start | bytes 3145732
  7.2 96.5 %all-gather.3.cloned.1.call-start = ((), (), s32[]{:S(2)}) async-start(), calls=%async_computation.4 | async-start | bytes 4456448 | tf_op jit(solution)/shard_map/all_gather | solution.py:149
  33.8 12.8 %copy-start.4 = (bf16[1,64,2048]{2,1,0:T(8,128)(2,1)S(1)}, bf16[1,64,2048]{2,1,0:T(8,128)(2,1)}, u32[]{:S(2)}) copy-start(bf16[1,64,2048]{2,1,0:T(8,128)(2,1)} %param.13) | copy-start | bytes 786436
  35.2 13.5 %copy-start.6 = (s32[1,64]{1,0:T(1,128)S(1)}, s32[1,64]{1,0:T(1,128)}, u32[]{:S(2)}) copy-start(s32[1,64]{1,0:T(1,128)} %param.18) | copy-start | bytes 772
  35.2 111.3 %all-to-all-start.1 = ((bf16[16,128,1,256]{3,1,2,0:T(8,128)(2,1)}), bf16[16,128,1,256]{3,1,2,0:T(8,128)(2,1)S(1)}, u32[]{:S(2)}, u32[]{:S(2)}) async-start(bf16[16,128,1,256]{3,1,2,0:T(8,128)(2,1)} %copy.89), calls=%async_computation.1 | async-start | bytes 2097152 | tf_op jit(solution)/shard_map/all_to_all | solution.py:24
  45.8 102.1 %all-gather.5.cloned.1.call-start = ((), (), s32[]{:S(2)}) async-start(), calls=%async_computation.5 | async-start | bytes 2228224 | tf_op jit(solution)/shard_map/all_gather | solution.py:157
  103.7 3.6 %copy-start.1 = (bf16[512,4096]{1,0:T(8,128)(2,1)S(1)}, bf16[512,4096]{1,0:T(8,128)(2,1)}, u32[]{:S(2)}) copy-start(bf16[512,4096]{1,0:T(8,128)(2,1)} %all-gather.3.cloned.1.call-done) | copy-start | bytes 12582916
  103.7 3.7 %copy-start.5 = (bf16[1,4096,128]{2,1,0:T(8,128)(2,1)S(1)}, bf16[1,4096,128]{2,1,0:T(8,128)(2,1)}, u32[]{:S(2)}) copy-start(bf16[1,4096,128]{2,1,0:T(8,128)(2,1)} %param.24) | copy-start | bytes 3145732
  109.4 2.0 copy-start.3
  109.4 156.7 %all-reduce.4.cloned.1.call-start = ((), (), s32[]{:S(2)}) async-start(), calls=%async_computation.3 | async-start | bytes 1179648 | tf_op jit(solution)/shard_map/psum | solution.py:112
  111.4 30.2 %copy-start.2 = (bf16[1,4,128,512]{3,2,1,0:T(8,128)(2,1)S(1)}, bf16[1,4,128,512]{3,2,1,0:T(8,128)(2,1)}, u32[]{:S(2)}) copy-start(bf16[1,4,128,512]{3,2,1,0:T(8,128)(2,1)} %param.17) | copy-start | bytes 1572868
  150.9 118.2 %all-to-all-start.2 = ((bf16[32,16,256]{2,1,0:T(8,128)(2,1)}), bf16[32,16,256]{2,1,0:T(8,128)(2,1)S(1)}, u32[]{:S(2)}, u32[]{:S(2)}) async-start(bf16[32,16,256]{2,1,0:T(8,128)(2,1)} %convolution_convert_fusion.1), calls=%async_computation.2 | async-start | bytes 524288 | tf_op jit(solution)/shard_map/all_to_all | solution.py:162
Sparse Core Ops, SparseCore 0:
  32.1 71.5 all-gather.2
  109.5 38.3 all-gather.4
  150.3 115.7 all-reduce.3
